TPU v7x, 256 devices: a whole 4x4x8 slice. The times are simulated.
256 devices in a mesh: heads: 32 (over z_hi, y, x), width: 8 (over z_lo, core).
Axes of the slice: x: 4, y: 4, z: 8 (z_hi: 2, z_lo: 4; z = z_hi * 4 + z_lo), core: 2. Of those that a mesh axis runs over, the one named last changes fastest.
Arguments:
- states: bfloat16 [1536, 6144], P('heads', 'width'), may hold values from -6 to 6
- segment_ids: int32 [1536], replicated, may hold values from 0 to 11, never falling along the last dimension, each value on 1 to 1344 neighbouring positions
- attn_gain: float32 [6144], P('width'), may hold values from 0.1 to 1.9
- attn_shift: float32 [6144], P('width'), may hold values from -3 to 3
- mlp_gain: float32 [6144], P('width'), may hold values from 0.1 to 1.9
- mlp_shift: float32 [6144], P('width'), may hold values from -3 to 3
- qkv_weight: bfloat16 [6144, 18432], P('width', 'heads'), may hold values from -0.078125 to 0.078125
- qkv_bias: float32 [18432], P('heads'), may hold values from -6 to 6
- dense_weight: bfloat16 [6144, 6144], P('heads', 'width'), may hold values from -0.078125 to 0.078125
- dense_bias: float32 [6144], P('width'), may hold values from -2 to 2
- up_weight: bfloat16 [6144, 24576], P('width', 'heads'), may hold values from -0.078125 to 0.078125
- up_bias: float32 [24576], P('heads'), may hold values from -3 to 3
- down_weight: bfloat16 [24576, 6144], P('heads', 'width'), may hold values from -0.0390625 to 0.0390625
- down_bias: float32 [6144], P('width'), may hold values from -2 to 2
Outputs:
- layer_out: bfloat16 [1536, 6144], P('heads', 'width')
- key_cache: bfloat16 [1536, 6144], P('width', 'heads')
- value_cache: bfloat16 [1536, 6144], P('width', 'heads')
Inputs may be any that keep to these rules, and one draw needn't show every extreme that they name: `segment_ids`: document numbers never fall along the tokens; each document has 1 to 1344 tokens and one has exactly 1344.
All inputs are finite; a program needn't handle non-finite values.
Results may differ from a plain program's by a relative error of at most 0.017.
Values may be sent and summed in bfloat16 or wider, within the bound.
No kernel may reach another device: no remote copies, remote signals or barrier semaphores. Data moves between devices by JAX's collectives and lax.ppermute only.
A program may use at most 64 MiB of HBM per device.

v0:
```python
import jax
import jax.numpy as jnp
from jax import lax
from jax.sharding import PartitionSpec as P

HD = 96
ROT = 24
D = 6144
norm_epsilon = 1e-05


def positions_of(segments):
    count = segments.shape[0]
    row_index = jnp.arange(count, dtype=jnp.int32)
    change = jnp.concatenate([jnp.ones((1,), bool), segments[1:] != segments[:-1]])
    first = lax.cummax(jnp.where(change, row_index, 0), axis=0)
    return (row_index - first).astype(jnp.float32)


def rotary(values, positions):
    half_rot = ROT // 2
    inverse = 10000.0 ** (-(jnp.arange(half_rot, dtype=jnp.float32) * 2.0 / ROT))
    angles = positions[:, None] * inverse[None, :]
    cosine = jnp.cos(angles)[:, None, :]
    sine_part = jnp.sin(angles)[:, None, :]
    first_half = values[..., :half_rot]
    second_half = values[..., half_rot:ROT]
    return jnp.concatenate(
        [
            first_half * cosine - second_half * sine_part,
            second_half * cosine + first_half * sine_part,
            values[..., ROT:],
        ],
        axis=-1,
    )


def on_device(
    states,
    segment_ids,
    attn_gain,
    attn_shift,
    mlp_gain,
    mlp_shift,
    qkv_weight,
    qkv_bias,
    dense_weight,
    dense_bias,
    up_weight,
    up_bias,
    down_weight,
    down_bias,
):
    floats = states.astype(jnp.float32)
    row_sums, square_sums = lax.psum((jnp.sum(floats, -1), jnp.sum(floats * floats, -1)), "width")
    row_mean = (row_sums / D)[:, None]
    row_var = (square_sums / D)[:, None] - row_mean * row_mean
    normed = ((floats - row_mean) * lax.rsqrt(row_var + norm_epsilon)).astype(jnp.bfloat16)
    qkv_cols = qkv_weight.shape[1]
    heads_dev = qkv_cols // (3 * HD)
    block_f = lax.all_gather(normed, "heads", axis=0, tiled=True).astype(jnp.float32)
    attn_in = (block_f * attn_gain + attn_shift).astype(jnp.bfloat16)
    mlp_in = (block_f * mlp_gain + mlp_shift).astype(jnp.bfloat16)
    projected = jnp.concatenate(
        [
            jnp.dot(attn_in, qkv_weight, preferred_element_type=jnp.float32),
            jnp.dot(mlp_in, up_weight, preferred_element_type=jnp.float32),
        ],
        axis=1,
    )
    qkv_part = projected[:, :qkv_cols]
    up_part = projected[:, qkv_cols:]
    all_tokens = projected.shape[0]
    own_rows = all_tokens // lax.axis_size("width")
    row_zero = lax.axis_index("width") * own_rows
    positions = positions_of(segment_ids)
    own_segments = lax.dynamic_slice_in_dim(segment_ids, row_zero, own_rows)
    own_index = row_zero + jnp.arange(own_rows, dtype=jnp.int32)
    score_scale = 1.0 / HD**0.5
    own_positions = lax.dynamic_slice_in_dim(positions, row_zero, own_rows)
    qkv_own, up_own = (
        lax.psum_scatter(qkv_part, "width", scatter_dimension=0, tiled=True),
        lax.psum_scatter(up_part, "width", scatter_dimension=0, tiled=True),
    )
    shaped = (qkv_own + qkv_bias).reshape(qkv_own.shape[0], heads_dev, 3, HD)
    queries = rotary(shaped[:, :, 0, :], own_positions).astype(jnp.bfloat16)
    keys_part = rotary(shaped[:, :, 1, :], own_positions).astype(jnp.bfloat16)
    values_part = shaped[:, :, 2, :].astype(jnp.bfloat16)
    width_cols = heads_dev * HD
    key_cache = keys_part.reshape(-1, width_cols)
    value_cache = values_part.reshape(-1, width_cols)
    run_max = jnp.full((heads_dev, own_rows), -1e30, jnp.float32)
    key_rows = lax.all_gather(key_cache, "width", axis=0, tiled=True)
    value_rows = lax.all_gather(value_cache, "width", axis=0, tiled=True)
    count = key_rows.shape[0]
    key_heads = key_rows.reshape(count, heads_dev, HD)
    value_heads = value_rows.reshape(count, heads_dev, HD)
    scores = (
        jnp.einsum("rhd,nhd->hrn", queries, key_heads, preferred_element_type=jnp.float32)
        * score_scale
    )
    key_index = jnp.arange(count, dtype=jnp.int32)
    allowed = (own_segments[:, None] == segment_ids[None, :]) & (
        key_index[None, :] <= own_index[:, None]
    )
    scores = jnp.where(allowed[None], scores, -1e30)
    new_max = jnp.maximum(run_max, jnp.max(scores, -1))
    weights = jnp.where(allowed[None], jnp.exp(scores - new_max[..., None]), 0.0)
    new_sum = jnp.sum(weights, -1)
    mixed = jnp.einsum(
        "hrn,nhd->hrd",
        weights.astype(jnp.bfloat16),
        value_heads,
        preferred_element_type=jnp.float32,
    )
    attended = (
        (mixed / new_sum[..., None])
        .transpose(1, 0, 2)
        .reshape(own_rows, heads_dev * HD)
        .astype(jnp.bfloat16)
    )
    attn_part = jnp.dot(
        lax.all_gather(attended, "width", axis=0, tiled=True),
        dense_weight,
        preferred_element_type=jnp.float32,
    )
    hidden = jax.nn.gelu(up_own + up_bias, approximate=False).astype(jnp.bfloat16)
    mlp_part = jnp.dot(
        lax.all_gather(hidden, "width", axis=0, tiled=True),
        down_weight,
        preferred_element_type=jnp.float32,
    )
    summed = lax.psum_scatter(
        attn_part.astype(jnp.bfloat16), "heads", scatter_dimension=0, tiled=True
    ).astype(jnp.float32) + lax.psum_scatter(
        mlp_part.astype(jnp.bfloat16), "heads", scatter_dimension=0, tiled=True
    ).astype(
        jnp.float32
    )
    layer_out = (floats + summed + dense_bias + down_bias).astype(jnp.bfloat16)
    return (layer_out, key_cache, value_cache)


def solution(mesh):
    in_specs = (
        P("heads", "width"),
        P(),
        P("width"),
        P("width"),
        P("width"),
        P("width"),
        P("width", "heads"),
        P("heads"),
        P("heads", "width"),
        P("width"),
        P("width", "heads"),
        P("heads"),
        P("heads", "width"),
        P("width"),
    )
    out_specs = (P("heads", "width"), P("width", "heads"), P("width", "heads"))
    return jax.shard_map(
        on_device, mesh=mesh, in_specs=in_specs, out_specs=out_specs, check_vma=False
    )
```

profile of v0, /device:TPU:2, one launch (start us, length us, event | category | flops | bytes accessed | tf_op | source)
XLA Modules:
  0.0 825.1 jit_solution(1113341373791377234)
XLA Ops:
  7.2 1.1 convert_reduce_fusion
  8.3 17.6 %all-reduce = (f32[48]{0:T(128)S(1)}, f32[48]{0:T(128)S(1)}) all-reduce(f32[48]{0:T(128)S(1)} %get-tuple-element.13, f32[48]{0:T(128)S(1)} %get-tuple-element.12), channel_id=1, replica_groups=mesh['heads'=32,'width'=8] {'width'}, use_global_device_ids=true, to_apply=%region_3.0 | all-reduce | flops 96 | bytes 768 | tf_op jit(solution)/shard_map/psum | solution.py:55
  26.0 1.6 fusion.41
  27.7 92.7 %all-gather.3.cloned.1.call-done = bf16[1536,768]{1,0:T(8,128)(2,1)} async-done(((bf16[48,768]{1,0:T(8,128)(2,1)}), bf16[1536,768]{1,0:T(8,128)(2,1)}) %all-gather.3.cloned.1.call-update) | async-done | bytes 2359312 | tf_op jit(solution)/shard_map/all_gather | solution.py:61
  120.4 5.8 fusion.5
  126.3 1.6 copy-done.10
  127.9 5.1 fusion.7
  133.1 0.6 copy-done.5
  134.0 0.3 reduce-window.9
  134.5 47.2 %reduce-scatter.9.cloned.1.call-done = f32[192,768]{1,0:T(8,128)} async-done(((f32[1536,768]{1,0:T(8,128)}), f32[192,768]{1,0:T(8,128)}) %reduce-scatter.9.cloned.1.call-update) | async-done | bytes 589840 | tf_op jit(solution)/shard_map/reduce_scatter | solution.py:83
  181.7 3.1 fusion.32
  185.0 0.1 multiply_cosine_fusion
  185.4 0.5 fusion.19
  185.8 49.9 %reduce-scatter.5.cloned.1.call-done = f32[192,576]{1,0:T(8,128)} async-done(((f32[1536,576]{1,0:T(8,128)}), f32[192,576]{1,0:T(8,128)}) %reduce-scatter.5.cloned.1.call-update) | async-done | bytes 442384 | tf_op jit(solution)/shard_map/reduce_scatter | solution.py:82
  235.8 1.1 broadcast_add_fusion
  236.8 0.2 copy.38
  237.3 0.8 copy.46
  238.3 0.8 subtract_convert_fusion.1
  239.5 17.0 %all_gather.16 = bf16[1536,192]{1,0:T(8,128)(2,1)S(1)} all-gather(bf16[192,192]{1,0:T(8,128)(2,1)S(1)} %copy.44), channel_id=1, replica_groups=mesh['heads'=32,'width'=8] {'width'}, dimensions={0}, use_global_device_ids=true | all-gather | bytes 663552 | tf_op jit(solution)/shard_map/all_gather | solution.py:93
  256.6 0.3 copy.45
  256.9 18.8 %all_gather.17 = bf16[1536,192]{1,0:T(8,128)(2,1)S(1)} all-gather(bf16[192,192]{1,0:T(8,128)(2,1)S(1)} %copy-done.2), channel_id=1, replica_groups=mesh['heads'=32,'width'=8] {'width'}, dimensions={0}, use_global_device_ids=true | all-gather | bytes 663552 | tf_op jit(solution)/shard_map/all_gather | solution.py:94
  275.7 0.3 copy.47
  275.9 1.7 fusion.55
  277.7 0.7 fusion.13
  278.4 0.7 fusion.27
  279.2 15.8 %all_gather.18 = bf16[1536,192]{1,0:T(8,128)(2,1)S(1)} all-gather(bf16[192,192]{1,0:T(8,128)(2,1)S(1)} %copy.48), channel_id=1, replica_groups=mesh['heads'=32,'width'=8] {'width'}, dimensions={0}, use_global_device_ids=true | all-gather | bytes 663552 | tf_op jit(solution)/shard_map/all_gather | solution.py:123
  295.0 2.2 convolution_convert_fusion.1
  297.3 1.2 copy-done.11
  298.5 5.1 convolution_convert_fusion
  303.6 252.6 %reduce-scatter.7.cloned.1.call-done = bf16[48,768]{1,0:T(8,128)(2,1)} async-done(((bf16[1536,768]{1,0:T(8,128)(2,1)}), bf16[48,768]{1,0:T(8,128)(2,1)}) %reduce-scatter.7.cloned.1.call-update) | async-done | bytes 73744 | tf_op jit(solution)/shard_map/reduce_scatter | solution.py:133
  556.2 260.5 %reduce-scatter.11.cloned.1.call-done = bf16[48,768]{1,0:T(8,128)(2,1)} async-done(((bf16[1536,768]{1,0:T(8,128)(2,1)}), bf16[48,768]{1,0:T(8,128)(2,1)}) %reduce-scatter.11.cloned.1.call-update) | async-done | bytes 73744 | tf_op jit(solution)/shard_map/reduce_scatter | solution.py:135
  816.7 1.6 fusion.45
  (62 shorter events, 2.2 us)
Async XLA Ops:
  7.2 113.2 %copy-start = (bf16[768,768]{1,0:T(8,128)(2,1)S(1)}, bf16[768,768]{1,0:T(8,128)(2,1)}, u32[]{:S(2)}) copy-start(bf16[768,768]{1,0:T(8,128)(2,1)} %param.24) | copy-start | bytes 3538948
  7.2 113.2 %all-gather.3.cloned.1.call-start = ((), (), s32[]{:S(2)}) async-start(), calls=%async_computation.4 | async-start | bytes 2433024 | tf_op jit(solution)/shard_map/all_gather | solution.py:61
  27.6 154.1 %reduce-scatter.9.cloned.1.call-start = ((), (), s32[]{:S(2)}) async-start(), calls=%async_computation.7 | async-start | bytes 5308416 | tf_op jit(solution)/shard_map/reduce_scatter | solution.py:83
  126.2 1.7 copy-start.10
  126.2 1.7 copy-start.12
  126.2 1.7 copy-start.13
  126.3 109.5 %reduce-scatter.5.cloned.1.call-start = ((), (), s32[]{:S(2)}) async-start(), calls=%async_computation.5 | async-start | bytes 4423680 | tf_op jit(solution)/shard_map/reduce_scatter | solution.py:82
  133.0 0.7 copy-start.5
  133.0 48.7 %copy-start.6 = (f32[768]{0:T(1024)S(1)}, f32[768]{0:T(1024)}, u32[]{:S(2)}) copy-start(f32[768]{0:T(1024)} %param.25) | copy-start | bytes 9220
  133.0 102.8 %copy-start.7 = (f32[576]{0:T(1024)S(1)}, f32[576]{0:T(1024)}, u32[]{:S(2)}) copy-start(f32[576]{0:T(1024)} %param.21) | copy-start | bytes 6916
  133.1 164.2 %all-gather.5.cloned.1.call-start = ((), (), s32[]{:S(2)}) async-start(), calls=%async_computation.8 | async-start | bytes 2654208 | tf_op jit(solution)/shard_map/all_gather | solution.py:129
  184.8 371.4 %reduce-scatter.7.cloned.1.call-start = ((), (), s32[]{:S(2)}) async-start(), calls=%async_computation.6 | async-start | bytes 2433024 | tf_op jit(solution)/shard_map/reduce_scatter | solution.py:133
  238.2 18.6 %copy-start.2 = (bf16[192,192]{1,0:T(8,128)(2,1)S(1)}, bf16[192,192]{1,0:T(8,128)(2,1)}, u32[]{:S(2)}) copy-start(bf16[192,192]{1,0:T(8,128)(2,1)} %copy.46) | copy-start | bytes 221188
  239.5 17.3 %copy-start.3 = (bf16[192,192]{1,0:T(8,128)(2,1)}, bf16[192,192]{1,0:T(8,128)(2,1)S(1)}, u32[]{:S(2)}) copy-start(bf16[192,192]{1,0:T(8,128)(2,1)S(1)} %copy.44) | copy-start | bytes 221188
  278.4 16.6 %copy-start.4 = (bf16[192,768]{1,0:T(8,128)(2,1)S(1)}, bf16[192,768]{1,0:T(8,128)(2,1)}, u32[]{:S(2)}) copy-start(bf16[192,768]{1,0:T(8,128)(2,1)} %param.22) | copy-start | bytes 884740
  297.2 1.3 copy-start.11
  297.2 519.4 %reduce-scatter.11.cloned.1.call-start = ((), (), s32[]{:S(2)}) async-start(), calls=%async_computation.9 | async-start | bytes 2433024 | tf_op jit(solution)/shard_map/reduce_scatter | solution.py:135
  303.6 513.1 %copy-start.1 = (bf16[48,768]{1,0:T(8,128)(2,1)S(1)}, bf16[48,768]{1,0:T(8,128)(2,1)}, u32[]{:S(2)}) copy-start(bf16[48,768]{1,0:T(8,128)(2,1)} %param.14) | copy-start | bytes 221188
  303.6 513.1 %copy-start.8 = (f32[768]{0:T(1024)S(1)}, f32[768]{0:T(1024)}, u32[]{:S(2)}) copy-start(f32[768]{0:T(1024)} %param.27) | copy-start | bytes 9220
  303.6 513.1 %copy-start.9 = (f32[768]{0:T(1024)S(1)}, f32[768]{0:T(1024)}, u32[]{:S(2)}) copy-start(f32[768]{0:T(1024)} %param.23) | copy-start | bytes 9220
Sparse Core Ops, SparseCore 0:
  27.7 92.6 all-gather.2
  126.4 55.2 reduce-scatter.8
  184.3 51.4 reduce-scatter.4
  237.4 44.4 all-gather.4
  297.4 258.7 reduce-scatter.6
  561.4 255.1 reduce-scatter.10
where the time goes:
time: 826 us; the launch traced here: 825 us
  waiting for transfers between devices  703 us (85%)
  blocking collectives  69.3 us (8%)
  matrix products  20.7 us (3%)
  between operations  14.3 us (2%)
  other arithmetic  11.4 us (1%)
    reduce_scatter x1, waiting for transfers between devices, on_device(): lax.psum_scatter(mlp_part.astype(jnp.bfloat16), 'heads', scatter_dimensio...  260 us
    reduce_scatter x1, waiting for transfers between devices, on_device(): lax.psum_scatter(attn_part.astype(jnp.bfloat16), 'heads', scatter_dimensi...  253 us
    all_gather x1, waiting for transfers between devices, on_device(): lax.all_gather(normed, 'heads', axis=0, tiled=True).astype(jnp.float32)  92.7 us
    reduce_scatter x1, waiting for transfers between devices, on_device(): lax.psum_scatter(qkv_part, 'width', scatter_dimension=0, tiled=True)  49.9 us
    reduce_scatter x1, waiting for transfers between devices, on_device(): lax.psum_scatter(up_part, 'width', scatter_dimension=0, tiled=True)  47.2 us
    all_gather x1, blocking collectives, on_device(): value_rows = lax.all_gather(value_cache, 'width', axis=0, tiled=True)  18.8 us
    psum x1, blocking collectives, on_device(): lax.psum((jnp.sum(floats, -1), jnp.sum(floats * floats, -1)), 'width')  17.6 us
    all_gather x1, blocking collectives, on_device(): key_rows = lax.all_gather(key_cache, 'width', axis=0, tiled=True)  17 us
  transfers between devices with their start and end apart: 6, of which 5 were waited for; matrix products, arithmetic and copies ran while one was open for 3% of the time, Pallas kernels for 0%

commit v1 on v0

--- a/solution.py
+++ b/solution.py
@@ -2,6 +2,7 @@
 import jax.numpy as jnp
 from jax import lax
 from jax.sharding import PartitionSpec as P
+from jax.lax import all_to_all, axis_size
 
 HD = 96
 ROT = 24
@@ -51,6 +52,13 @@
     down_weight,
     down_bias,
 ):
+
+    def find_the_members_all(incoming_x, along_dim):
+        z1 = axis_size("heads")
+        val2 = jnp.stack(z1 * [incoming_x], 0)
+        t1 = all_to_all(val2, "heads", split_axis=0, concat_axis=0)
+        return jnp.concatenate(t1, along_dim)
+
     floats = states.astype(jnp.float32)
     row_sums, square_sums = lax.psum((jnp.sum(floats, -1), jnp.sum(floats * floats, -1)), "width")
     row_mean = (row_sums / D)[:, None]
@@ -58,7 +66,7 @@
     normed = ((floats - row_mean) * lax.rsqrt(row_var + norm_epsilon)).astype(jnp.bfloat16)
     qkv_cols = qkv_weight.shape[1]
     heads_dev = qkv_cols // (3 * HD)
-    block_f = lax.all_gather(normed, "heads", axis=0, tiled=True).astype(jnp.float32)
+    block_f = find_the_members_all(normed, 0).astype(jnp.float32)
     attn_in = (block_f * attn_gain + attn_shift).astype(jnp.bfloat16)
     mlp_in = (block_f * mlp_gain + mlp_shift).astype(jnp.bfloat16)
     projected = jnp.concatenate(

time: 826 us -> 798 us (0.966)
  waiting for transfers between devices: 703 us -> 614 us
  blocking collectives: 69.3 us -> 134 us
    all_gather x1 -> x0, waiting for transfers between devices: 92.7 us -> none  [on_device(): lax.all_gather(normed, 'heads', axis=0, tiled=True).astype(jnp.float32)]
    all_to_all x0 -> x1, blocking collectives: none -> 64.9 us  [find_the_members_all(): t1 = all_to_all(val2, 'heads', split_axis=0, concat_axis=0)]
  transfers between devices with their start and end apart: 6 -> 5, of which waited for: 5 -> 4; matrix products, arithmetic and copies ran while one was open for 3% -> 3% of each run, Pallas kernels for 0% -> 0%
where the time goes in v1:
time: 798 us
  waiting for transfers between devices  614 us (77%)
  blocking collectives  134 us (17%)
  matrix products  19 us (2%)
  between operations  14 us (2%)
  other arithmetic  10.7 us (1%)
    reduce_scatter x1, waiting for transfers between devices, on_device(): lax.psum_scatter(mlp_part.astype(jnp.bfloat16), 'heads', scatter_dimensio...  260 us
    reduce_scatter x1, waiting for transfers between devices, on_device(): lax.psum_scatter(attn_part.astype(jnp.bfloat16), 'heads', scatter_dimensi...  252 us
    all_to_all x1, blocking collectives, find_the_members_all(): t1 = all_to_all(val2, 'heads', split_axis=0, concat_axis=0)  64.9 us
    reduce_scatter x1, waiting for transfers between devices, on_device(): lax.psum_scatter(up_part, 'width', scatter_dimension=0, tiled=True)  51.4 us
    reduce_scatter x1, waiting for transfers between devices, on_device(): lax.psum_scatter(qkv_part, 'width', scatter_dimension=0, tiled=True)  49.9 us
    all_gather x1, blocking collectives, on_device(): value_rows = lax.all_gather(value_cache, 'width', axis=0, tiled=True)  19 us
    psum x1, blocking collectives, on_device(): lax.psum((jnp.sum(floats, -1), jnp.sum(floats * floats, -1)), 'width')  17.6 us
    all_gather x1, blocking collectives, on_device(): key_rows = lax.all_gather(key_cache, 'width', axis=0, tiled=True)  16.9 us
  transfers between devices with their start and end apart: 5, of which 4 were waited for; matrix products, arithmetic and copies ran while one was open for 3% of the time, Pallas kernels for 0%

profile of v1, /device:TPU:2, one launch (start us, length us, event | category | flops | bytes accessed | tf_op | source)
XLA Modules:
  0.0 797.8 jit_solution(13250024622613973606)
XLA Ops:
  7.2 1.1 convert_reduce_fusion
  8.3 17.6 %all-reduce = (f32[48]{0:T(128)S(1)}, f32[48]{0:T(128)S(1)}) all-reduce(f32[48]{0:T(128)S(1)} %get-tuple-element.13, f32[48]{0:T(128)S(1)} %get-tuple-element.12), channel_id=1, replica_groups=mesh['heads'=32,'width'=8] {'width'}, use_global_device_ids=true, to_apply=%region_3.0 | all-reduce | flops 96 | bytes 768 | tf_op jit(solution)/shard_map/psum | solution.py:63
  26.0 1.0 fusion.41
  27.0 0.2 stack.2
  27.1 64.9 %all_to_all.5 = bf16[32,48,768]{2,1,0:T(8,128)(2,1)S(1)} all-to-all(bf16[32,48,768]{2,1,0:T(8,128)(2,1)S(1)} %stack.2), channel_id=1, replica_groups=mesh['heads'=32,'width'=8] {'heads'}, dimensions={0} | all-to-all | bytes 4718592 | tf_op jit(solution)/shard_map/all_to_all | solution.py:59
  92.1 4.2 fusion.5
  96.3 0.6 copy-done.13
  96.9 5.1 fusion.7
  102.1 0.6 copy-done.5
  103.0 0.3 reduce-window.9
  103.5 51.4 %reduce-scatter.9.cloned.1.call-done = f32[192,768]{1,0:T(8,128)} async-done(((f32[1536,768]{1,0:T(8,128)}), f32[192,768]{1,0:T(8,128)}) %reduce-scatter.9.cloned.1.call-update) | async-done | bytes 589840 | tf_op jit(solution)/shard_map/reduce_scatter | solution.py:91
  154.9 3.1 fusion.32
  158.6 0.5 fusion.19
  159.1 49.9 %reduce-scatter.5.cloned.1.call-done = f32[192,576]{1,0:T(8,128)} async-done(((f32[1536,576]{1,0:T(8,128)}), f32[192,576]{1,0:T(8,128)}) %reduce-scatter.5.cloned.1.call-update) | async-done | bytes 442384 | tf_op jit(solution)/shard_map/reduce_scatter | solution.py:90
  209.0 1.1 broadcast_add_fusion
  210.0 0.2 copy.38
  210.5 0.8 copy.46
  211.5 0.8 subtract_convert_fusion.1
  212.7 16.9 %all_gather.12 = bf16[1536,192]{1,0:T(8,128)(2,1)S(1)} all-gather(bf16[192,192]{1,0:T(8,128)(2,1)S(1)} %copy.44), channel_id=1, replica_groups=mesh['heads'=32,'width'=8] {'width'}, dimensions={0}, use_global_device_ids=true | all-gather | bytes 663552 | tf_op jit(solution)/shard_map/all_gather | solution.py:101
  229.6 0.3 copy.45
  229.9 19.0 %all_gather.13 = bf16[1536,192]{1,0:T(8,128)(2,1)S(1)} all-gather(bf16[192,192]{1,0:T(8,128)(2,1)S(1)} %copy-done.2), channel_id=1, replica_groups=mesh['heads'=32,'width'=8] {'width'}, dimensions={0}, use_global_device_ids=true | all-gather | bytes 663552 | tf_op jit(solution)/shard_map/all_gather | solution.py:102
  248.9 0.3 copy.47
  249.1 1.7 fusion.55
  250.9 0.7 fusion.13
  251.6 0.7 fusion.27
  252.4 15.9 %all_gather.14 = bf16[1536,192]{1,0:T(8,128)(2,1)S(1)} all-gather(bf16[192,192]{1,0:T(8,128)(2,1)S(1)} %copy.48), channel_id=1, replica_groups=mesh['heads'=32,'width'=8] {'width'}, dimensions={0}, use_global_device_ids=true | all-gather | bytes 663552 | tf_op jit(solution)/shard_map/all_gather | solution.py:131
  268.3 2.2 convolution_convert_fusion.1
  270.6 1.2 copy-done.10
  271.8 5.1 convolution_convert_fusion
  276.9 252.3 %reduce-scatter.7.cloned.1.call-done = bf16[48,768]{1,0:T(8,128)(2,1)} async-done(((bf16[1536,768]{1,0:T(8,128)(2,1)}), bf16[48,768]{1,0:T(8,128)(2,1)}) %reduce-scatter.7.cloned.1.call-update) | async-done | bytes 73744 | tf_op jit(solution)/shard_map/reduce_scatter | solution.py:141
  529.2 260.5 %reduce-scatter.11.cloned.1.call-done = bf16[48,768]{1,0:T(8,128)(2,1)} async-done(((bf16[1536,768]{1,0:T(8,128)(2,1)}), bf16[48,768]{1,0:T(8,128)(2,1)}) %reduce-scatter.11.cloned.1.call-update) | async-done | bytes 73744 | tf_op jit(solution)/shard_map/reduce_scatter | solution.py:143
  789.7 1.6 fusion.45
  (63 shorter events, 2.3 us)
Async XLA Ops:
  7.2 84.9 %copy-start = (bf16[768,768]{1,0:T(8,128)(2,1)S(1)}, bf16[768,768]{1,0:T(8,128)(2,1)}, u32[]{:S(2)}) copy-start(bf16[768,768]{1,0:T(8,128)(2,1)} %param.24) | copy-start | bytes 3538948
  7.2 147.7 %reduce-scatter.9.cloned.1.call-start = ((), (), s32[]{:S(2)}) async-start(), calls=%async_computation.7 | async-start | bytes 5308416 | tf_op jit(solution)/shard_map/reduce_scatter | solution.py:91
  27.1 64.9 %copy-start.11 = (f32[768]{0:T(1024)S(1)}, f32[768]{0:T(1024)}, u32[]{:S(2)}) copy-start(f32[768]{0:T(1024)} %param.19) | copy-start | bytes 9220
  27.1 64.9 %copy-start.12 = (f32[768]{0:T(1024)S(1)}, f32[768]{0:T(1024)}, u32[]{:S(2)}) copy-start(f32[768]{0:T(1024)} %param.18) | copy-start | bytes 9220
  96.2 0.7 copy-start.13
  96.2 0.7 copy-start.14
  96.2 112.7 %reduce-scatter.5.cloned.1.call-start = ((), (), s32[]{:S(2)}) async-start(), calls=%async_computation.5 | async-start | bytes 4423680 | tf_op jit(solution)/shard_map/reduce_scatter | solution.py:90
  102.0 0.7 copy-start.5
  102.0 52.9 %copy-start.6 = (f32[768]{0:T(1024)S(1)}, f32[768]{0:T(1024)}, u32[]{:S(2)}) copy-start(f32[768]{0:T(1024)} %param.25) | copy-start | bytes 9220
  102.0 106.9 %copy-start.7 = (f32[576]{0:T(1024)S(1)}, f32[576]{0:T(1024)}, u32[]{:S(2)}) copy-start(f32[576]{0:T(1024)} %param.21) | copy-start | bytes 6916
  102.1 168.5 %all-gather.2.cloned.1.call-start = ((), (), s32[]{:S(2)}) async-start(), calls=%async_computation.8 | async-start | bytes 2654208 | tf_op jit(solution)/shard_map/all_gather | solution.py:137
  158.0 371.2 %reduce-scatter.7.cloned.1.call-start = ((), (), s32[]{:S(2)}) async-start(), calls=%async_computation.6 | async-start | bytes 2433024 | tf_op jit(solution)/shard_map/reduce_scatter | solution.py:141
  211.4 18.5 %copy-start.2 = (bf16[192,192]{1,0:T(8,128)(2,1)S(1)}, bf16[192,192]{1,0:T(8,128)(2,1)}, u32[]{:S(2)}) copy-start(bf16[192,192]{1,0:T(8,128)(2,1)} %copy.46) | copy-start | bytes 221188
  212.7 17.2 %copy-start.3 = (bf16[192,192]{1,0:T(8,128)(2,1)}, bf16[192,192]{1,0:T(8,128)(2,1)S(1)}, u32[]{:S(2)}) copy-start(bf16[192,192]{1,0:T(8,128)(2,1)S(1)} %copy.44) | copy-start | bytes 221188
  251.6 16.7 %copy-start.4 = (bf16[192,768]{1,0:T(8,128)(2,1)S(1)}, bf16[192,768]{1,0:T(8,128)(2,1)}, u32[]{:S(2)}) copy-start(bf16[192,768]{1,0:T(8,128)(2,1)} %param.22) | copy-start | bytes 884740
  270.5 1.3 copy-start.10
  270.5 519.1 %reduce-scatter.11.cloned.1.call-start = ((), (), s32[]{:S(2)}) async-start(), calls=%async_computation.9 | async-start | bytes 2433024 | tf_op jit(solution)/shard_map/reduce_scatter | solution.py:143
  276.9 512.8 %copy-start.1 = (bf16[48,768]{1,0:T(8,128)(2,1)S(1)}, bf16[48,768]{1,0:T(8,128)(2,1)}, u32[]{:S(2)}) copy-start(bf16[48,768]{1,0:T(8,128)(2,1)} %param.14) | copy-start | bytes 221188
  276.9 512.8 %copy-start.8 = (f32[768]{0:T(1024)S(1)}, f32[768]{0:T(1024)}, u32[]{:S(2)}) copy-start(f32[768]{0:T(1024)} %param.27) | copy-start | bytes 9220
  276.9 512.8 %copy-start.9 = (f32[768]{0:T(1024)S(1)}, f32[768]{0:T(1024)}, u32[]{:S(2)}) copy-start(f32[768]{0:T(1024)} %param.23) | copy-start | bytes 9220
Sparse Core Ops, SparseCore 0:
  96.4 58.5 reduce-scatter.8
  157.5 51.4 reduce-scatter.4
  210.8 44.6 all-gather.1
  270.6 258.5 reduce-scatter.6
  534.4 255.1 reduce-scatter.10
